TPU v7x, 32 devices: a whole 2x2x4 slice. The times are simulated.
32 devices in a mesh: seq: 8 (over y, x, core), panel: 4 (over z).
Axes of the slice: x: 2, y: 2, z: 4, core: 2. Of those that a mesh axis runs over, the one named last changes fastest.
Arguments:
- tokens: bfloat16 [2048, 1024], P('seq', 'panel'), may hold values from -6 to 6
- cotangent: bfloat16 [2048, 1024], P('seq', 'panel'), may hold values from -6 to 6
- in_weight: bfloat16 [3, 1024, 1024], P(None, None, 'panel'), may hold values from -0.1875 to 0.1875
- short_kernel: float32 [3, 3, 1024], P(None, None, 'panel'), may hold values from -1 to 1
- skip_gain: float32 [1024], P('panel'), may hold values from 0.5 to 1.5
- long_filter: float32 [2048, 1024], P('seq', 'panel'), may hold values from -1.25 to 1.25
- out_weight: bfloat16 [1024, 1024], P('panel'), may hold values from -0.1875 to 0.1875
Outputs:
- block_out: bfloat16 [2048, 1024], P('seq', 'panel')
- token_grad: bfloat16 [2048, 1024], P('seq', 'panel')
All inputs are finite; a program needn't handle non-finite values.
Results may differ from a plain program's by a relative error of at most 0.007.
Values may be sent and summed in bfloat16 or wider, within the bound.
No kernel may reach another device: no remote copies, remote signals or barrier semaphores. Data moves between devices by JAX's collectives and lax.ppermute only.
A program may use at most 64 MiB of HBM per device.

v0:
```python
import math
import jax
import jax.numpy as jnp
import numpy as np
from jax import lax
from jax.sharding import PartitionSpec as P

HIGHEST = lax.Precision.HIGHEST
STAGE_A_PRECISION = lax.Precision.HIGH
STAGE_B_PRECISION = lax.Precision.HIGH
WIRE = jnp.bfloat16


def shifted(value, axis, steps):
    count = lax.axis_size(axis)
    initial, last = (max(0, -steps), min(count, count - steps))
    return lax.ppermute(value, axis, [(source, source + steps) for source in range(initial, last)])


def panel_parts(value):
    count = lax.axis_size("panel")
    me = lax.axis_index("panel")
    parts = [(value, me)]
    for k in range(1, count):
        moved = lax.ppermute(value, "panel", [(i, (i + k) % count) for i in range(count)])
        parts.append((moved, (me + count - k) % count))
    return parts


def panel_reduce_scatter(block_of):
    count = lax.axis_size("panel")
    me = lax.axis_index("panel")
    total = block_of(me)
    for k in range(1, count):
        sent = block_of((me + k) % count).astype(jnp.bfloat16)
        total = total + lax.ppermute(
            sent, "panel", [(i, (i + k) % count) for i in range(count)]
        ).astype(jnp.float32)
    return total.astype(jnp.bfloat16)


def phase(numer, period):
    return 2.0 * math.pi / period * (numer % period).astype(jnp.float32)


def transform_tables(shard_count, row_count):
    length = shard_count * row_count
    branch = jnp.arange(2, dtype=jnp.int32)
    shard = jnp.arange(shard_count, dtype=jnp.int32)
    row = jnp.arange(row_count, dtype=jnp.int32)
    small_shard, small_row = (np.arange(shard_count), np.arange(row_count))
    small_branch = np.arange(2)
    theta = (
        -2.0
        * math.pi
        / (2 * shard_count)
        * (
            (
                (2 * small_shard[:, None] * small_shard[None, :])[None]
                + small_branch[:, None, None] * small_shard[None, None, :]
            )
            % (2 * shard_count)
        )
    )
    stage_a_np = np.stack([np.cos(theta), np.sin(theta)], axis=1)
    stage_a = jnp.asarray(stage_a_np, dtype=jnp.float32)
    phi = (
        -2.0
        * math.pi
        / (2 * length)
        * (
            (
                (2 * small_shard[:, None] * small_row[None, :])[None]
                + small_branch[:, None, None] * small_row[None, :][None]
            )
            % (2 * length)
        )
    )
    twiddle = (jnp.asarray(np.cos(phi), jnp.float32), jnp.asarray(np.sin(phi), jnp.float32))
    psi = -phase(row[:, None] * row[None, :], row_count)
    cos_b, sin_b = (jnp.cos(psi), jnp.sin(psi))
    stage_b = jnp.stack([jnp.stack([cos_b, sin_b], axis=1), jnp.stack([-sin_b, cos_b], axis=1)])
    stage_a_inv = jnp.asarray(stage_a_np * (0.5 / length), dtype=jnp.float32)
    return (stage_a, twiddle, stage_b, stage_a_inv)


def complex_scale(value, cos_part, sin_part, axis):
    real_part = lax.index_in_dim(value, 0, axis, keepdims=False)
    imag_part = lax.index_in_dim(value, 1, axis, keepdims=False)
    return jnp.stack(
        [real_part * cos_part - imag_part * sin_part, real_part * sin_part + imag_part * cos_part],
        axis=axis,
    )


def to_columns(rows, wire=jnp.float32):
    shard_count = lax.axis_size("seq")
    batch, row_count, _ = rows.shape
    columns = lax.all_to_all(
        jnp.swapaxes(rows, 1, 2).astype(wire), "seq", split_axis=1, concat_axis=2, tiled=True
    ).astype(jnp.float32)
    return columns.reshape(batch, columns.shape[1], shard_count, row_count)


def to_rows(columns, wire=jnp.float32):
    batch, chan_count, shard_count, row_count = columns.shape
    rows = lax.all_to_all(
        columns.astype(wire), "seq", split_axis=2, concat_axis=1, tiled=True
    ).astype(jnp.float32)
    return jnp.swapaxes(rows.reshape(batch, shard_count * chan_count, row_count), 1, 2)


def forward_spectrum(columns, tables):
    stage_a, twiddle, stage_b, _ = tables
    spread = jnp.einsum("erkp,bcpm->bcerkm", stage_a, columns, precision=STAGE_A_PRECISION)
    spread = complex_scale(spread, twiddle[0], twiddle[1], 3)
    return jnp.einsum("bcerkm,rmsq->bceskq", spread, stage_b, precision=STAGE_B_PRECISION)


def inverse_spectrum(spectrum, tables):
    _, twiddle, stage_b, stage_a_inv = tables
    spread = jnp.einsum("bceskq,rmsq->bcerkm", spectrum, stage_b, precision=STAGE_B_PRECISION)
    spread = complex_scale(spread, twiddle[0], -twiddle[1], 3)
    return jnp.einsum("erkp,bcerkm->bcpm", stage_a_inv, spread, precision=STAGE_A_PRECISION)


def local(tokens, cotangent, in_weight, short_kernel, skip_gain, long_filter, out_weight):
    row_count = tokens.shape[0]
    tap_count = short_kernel.shape[0]
    shard_count = lax.axis_size("seq")
    tables = transform_tables(shard_count, row_count)
    filt_spec = forward_spectrum(to_columns(long_filter[None]), tables)
    width = tokens.shape[1]
    projected = 0.0
    for part, source in panel_parts(tokens):
        projected = projected + jnp.einsum(
            "td,jdc->jtc",
            part,
            lax.dynamic_slice_in_dim(in_weight, source * width, width, axis=1),
            preferred_element_type=jnp.float32,
        )
    grad_gated = 0.0
    for part, source in panel_parts(cotangent):
        grad_gated = grad_gated + lax.dot_general(
            part,
            lax.dynamic_slice_in_dim(out_weight, source * width, width, axis=1),
            (((1,), (1,)), ((), ())),
            preferred_element_type=jnp.float32,
        )
    projected = projected.astype(jnp.bfloat16)
    before = shifted(projected[:, row_count - (tap_count - 1) :, :], "seq", 1)
    extended = jnp.concatenate([before, projected], axis=1).astype(jnp.float32)
    filtered = short_kernel[0][:, None, :] * extended[:, tap_count - 1 :, :]
    for tap_index in range(1, tap_count):
        filtered = (
            filtered
            + short_kernel[tap_index][:, None, :]
            * extended[:, tap_count - 1 - tap_index : tap_count - 1 - tap_index + row_count, :]
        )
    gate_out, gate_in, value_path = (filtered[0], filtered[1], filtered[2])
    signal = value_path * gate_in
    grad_state = grad_gated * gate_out
    spectra = forward_spectrum(to_columns(jnp.stack([signal, grad_state]), WIRE), tables)
    filt_real, filt_imag = (filt_spec[:, :, :, 0], filt_spec[:, :, :, 1])
    sig_real, sig_imag = (spectra[0:1, :, :, 0], spectra[0:1, :, :, 1])
    grad_real, grad_imag = (spectra[1:2, :, :, 0], spectra[1:2, :, :, 1])
    product = jnp.concatenate(
        [
            jnp.stack(
                [
                    sig_real * filt_real - sig_imag * filt_imag,
                    sig_real * filt_imag + sig_imag * filt_real,
                ],
                axis=3,
            ),
            jnp.stack(
                [
                    grad_real * filt_real + grad_imag * filt_imag,
                    grad_imag * filt_real - grad_real * filt_imag,
                ],
                axis=3,
            ),
        ]
    )
    convolved = to_rows(inverse_spectrum(product, tables), WIRE)
    conv_state = convolved[0] + skip_gain[None, :] * signal
    grad_signal = convolved[1] + skip_gain[None, :] * grad_state
    gated_state = (conv_state * gate_out).astype(jnp.bfloat16)
    block_out = panel_reduce_scatter(
        lambda dest: jnp.dot(
            gated_state,
            lax.dynamic_slice_in_dim(out_weight, dest * width, width, axis=1),
            preferred_element_type=jnp.float32,
        )
    )
    grad_gate_out = grad_gated * conv_state
    grad_value = grad_signal * gate_in
    grad_gate_in = grad_signal * value_path
    upstream = jnp.stack([grad_gate_out, grad_gate_in, grad_value])
    after_rim = shifted(upstream[:, : tap_count - 1, :], "seq", -1)
    widened = jnp.concatenate([upstream, after_rim], axis=1)
    grad_projected = short_kernel[0][:, None, :] * widened[:, :row_count, :]
    for tap_index in range(1, tap_count):
        grad_projected = (
            grad_projected
            + short_kernel[tap_index][:, None, :] * widened[:, tap_index : tap_index + row_count, :]
        )
    grad_projected = grad_projected.astype(jnp.bfloat16)
    token_grad = panel_reduce_scatter(
        lambda dest: jnp.einsum(
            "jtc,jdc->td",
            grad_projected,
            lax.dynamic_slice_in_dim(in_weight, dest * width, width, axis=1),
            preferred_element_type=jnp.float32,
        )
    )
    return (block_out, token_grad)


def solution(mesh):
    placed = (
        P("seq", "panel"),
        P("seq", "panel"),
        P(None, None, "panel"),
        P(None, None, "panel"),
        P("panel"),
        P("seq", "panel"),
        P("panel", None),
    )
    return jax.shard_map(
        local,
        mesh=mesh,
        in_specs=placed,
        out_specs=(P("seq", "panel"), P("seq", "panel")),
        check_vma=False,
    )
```

profile of v0, /device:TPU:9, one launch (start us, length us, event | category | flops | bytes accessed | tf_op | source)
XLA Modules:
  0.0 95.5 jit_solution(1160381794692749451)
XLA Ops:
  0.7 1.3 %collective-permute-start = (bf16[256,256]{1,0:T(8,128)(2,1)}, bf16[256,256]{1,0:T(8,128)(2,1)}, u32[]{:S(2)}, u32[]{:S(2)}) collective-permute-start(bf16[256,256]{1,0:T(8,128)(2,1)} %param.11), channel_id=1, source_target_pairs={{0,1},{1,2},{2,3},{3,0},{4,5},{5,6},{6,7},{7,4},{8,9},{9,10},{10,1... | collective-permute-start | bytes 393224 | tf_op jit(solution)/shard_map/ppermute | solution.py:25
  2.2 2.3 %collective-permute-start.1 = (bf16[256,256]{1,0:T(8,128)(2,1)}, bf16[256,256]{1,0:T(8,128)(2,1)}, u32[]{:S(2)}, u32[]{:S(2)}) collective-permute-start(bf16[256,256]{1,0:T(8,128)(2,1)} %param.11), channel_id=1, source_target_pairs={{0,2},{1,3},{2,0},{3,1},{4,6},{5,7},{6,4},{7,5},{8,10},{9,11},{10,... | collective-permute-start | bytes 393224 | tf_op jit(solution)/shard_map/ppermute | solution.py:25
  6.0 1.8 %copy.64 = f32[1,256,256]{1,0,2:T(1,128)} copy(f32[1,256,256]{2,1,0:T(8,128)} %bitcast.216) | data formatting | bytes 524288 | tf_op jit(solution)/shard_map/broadcast_in_dim | solution.py:132
  7.7 5.8 %all-to-all-start.1 = ((f32[1,256,256]{2,0,1:T(1,128)}), f32[1,256,256]{2,0,1:T(1,128)S(1)}, u32[]{:S(2)}, u32[]{:S(2)}) async-start(f32[1,256,256]{2,0,1:T(1,128)} %bitcast.34), calls=%async_computation.1 | async-start | bytes 524288 | tf_op jit(solution)/shard_map/all_to_all | solution.py:99
  13.5 1.0 %fusion.88 = f32[256,1,256]{2,0,1:T(8,128)S(1)} fusion(), kind=kLoop, calls=%fused_computation.124 | loop fusion | flops 1048576 | bytes 262144 | tf_op jit(solution)/shard_map/neg | solution.py:82
  14.5 1.0 %fusion.86 = (f32[256,1,256]{2,0,1:T(8,128)S(1)}, f32[256,1,256]{2,0,1:T(8,128)S(1)}) fusion(), kind=kLoop, calls=%fused_computation.122 | loop fusion | flops 983040 | bytes 524288 | tf_op jit(solution)/shard_map/sin | solution.py:81
  16.3 1.9 %fusion.98 = f32[256,256]{0,1:T(8,128)} fusion(bf16[256,256]{1,0:T(8,128)(2,1)} %param.12, bf16[256,1024]{1,0:T(8,128)(2,1)} %param.17, s32[]{:T(128)S(6)} %select_n.85), kind=kOutput, calls=%fused_computation.134 | convolution fusion | flops 33554432 | bytes 524292 | tf_op jit(solution)/shard_map/dot_general | solution.py:144
  18.5 1.1 %maximum_bitcast_fusion.2 = (f32[1,256,2,256]{3,1,0,2:T(8,128)}, f32[1,256,2,256]{3,1,0,2:T(8,128)}) fusion(f32[256,1,256]{2,0,1:T(8,128)S(1)} %get-tuple-element.25, f32[256,1,256]{2,0,1:T(8,128)S(1)} %get-tuple-element.26, f32[256,1,256]{2,0,1:T(8,128)S(1)} %fusion.88), kind=kLoop, calls=%fused_computation.62 | loop fusion | flops 262144 | bytes 1835008 | tf_op jit(solution)/shard_map/stack | solution.py:82
  20.1 1.2 %convolution_add_fusion.1 = f32[3,256,256]{1,2,0:T(8,128)S(1)} fusion(f32[3,256,256]{1,2,0:T(8,128)S(1)} %fusion.51, bf16[3,1024,256]{2,1,0:T(8,128)(2,1)S(1)} %copy-done, s32[]{:T(128)S(6)} %select_n.87, bf16[256,256]{1,0:T(8,128)(2,1)} %collective-permute-done), kind=kOutput, calls=%fused_computation.19 | convolution fusion | flops 100859904 | bytes 2097156 | tf_op jit(solution)/shard_map/td,jdc->jtc/dot_general | solution.py:136
  21.3 1.2 %fusion.44 = f32[3,256,256]{1,2,0:T(8,128)S(1)} fusion(bf16[3,1024,256]{2,1,0:T(8,128)(2,1)S(1)} %copy-done, s32[]{:T(128)S(6)} %select_n.91, bf16[256,256]{1,0:T(8,128)(2,1)} %collective-permute-done.2), kind=kOutput, calls=%fused_computation.75 | convolution fusion | flops 100663296 | bytes 1310724 | tf_op jit(solution)/shard_map/td,jdc->jtc/dot_general | solution.py:136
  22.6 1.2 %fusion.21 = bf16[3,256,256]{2,1,0:T(8,128)(2,1)S(1)} fusion(f32[3,256,256]{1,2,0:T(8,128)S(1)} %fusion.44, f32[3,256,256]{1,2,0:T(8,128)S(1)} %convolution_add_fusion.1, bf16[3,1024,256]{2,1,0:T(8,128)(2,1)S(1)} %copy-done, s32[]{:T(128)S(6)} %select_n.89, bf16[256,256]{1,0:T(8,128)(2,1)} %collective-permute-done.1), kind=kOutput, calls=%fused_computation.22 | convolution fusion | flops 101253120 | bytes 2490372 | tf_op jit(solution)/shard_map/td,jdc->jtc/dot_general | solution.py:136
  23.8 3.8 %collective-permute-start.3 = (bf16[3,2,256]{2,1,0:T(2,128)(2,1)S(1)}, bf16[3,2,256]{2,1,0:T(2,128)(2,1)S(1)}, u32[]{:S(2)}, u32[]{:S(2)}) collective-permute-start(bf16[3,2,256]{2,1,0:T(2,128)(2,1)S(1)} %slice.111), channel_id=1, source_target_pairs={{0,4},{4,8},{8,12},{12,16},{16,20},{20,24},{24,28},{1,5},{5,9},{9,... | collective-permute-start | bytes 9224 | tf_op jit(solution)/shard_map/ppermute | solution.py:17
  27.6 1.1 %convolution_add_fusion.3 = f32[256,256]{0,1:T(8,128)S(1)} fusion(f32[256,256]{0,1:T(8,128)S(1)} %copy-done.9, bf16[256,256]{1,0:T(8,128)(2,1)} %collective-permute-done.4, bf16[256,1024]{1,0:T(8,128)(2,1)S(1)} %copy-done.7, s32[]{:T(128)S(6)} %select_n.87), kind=kOutput, calls=%fused_computation.31 | convolution fusion | flops 33619968 | bytes 786436 | tf_op jit(solution)/shard_map/dot_general | solution.py:144
  28.8 1.1 %fusion.90 = f32[256,256]{0,1:T(8,128)S(1)} fusion(bf16[256,256]{1,0:T(8,128)(2,1)} %collective-permute-done.6, bf16[256,1024]{1,0:T(8,128)(2,1)S(1)} %copy-done.7, s32[]{:T(128)S(6)} %select_n.91), kind=kOutput, calls=%fused_computation.126 | convolution fusion | flops 33554432 | bytes 524292 | tf_op jit(solution)/shard_map/dot_general | solution.py:144
  31.9 4.2 %all-to-all-start = ((bf16[2,256,256]{2,0,1:T(2,128)(2,1)}), bf16[2,256,256]{2,0,1:T(2,128)(2,1)}, u32[]{:S(2)}, u32[]{:S(2)}) async-start(bf16[2,256,256]{2,0,1:T(2,128)(2,1)} %copy.34), calls=%async_computation | async-start | bytes 524288 | tf_op jit(solution)/shard_map/all_to_all | solution.py:99
  37.9 1.1 %convolution_bitcast_fusion.1 = f32[1,32,2,2,8,256]{5,1,4,2,0,3:T(8,128)S(1)} fusion(f32[32,2,2,8,256]{4,3,0,2,1:T(8,128)S(1)} %maximum_bitcast_fusion.1, f32[1,256,2,256]{3,1,0,2:T(8,128)S(1)} %copy-done.3, f32[1,256,2,256]{3,1,0,2:T(8,128)S(1)} %copy-done.1), kind=kOutput, calls=%fused_computation.15 | convolution fusion | flops 805568512 | bytes 3145728 | tf_op jit(solution)/shard_map/bcerkm,rmsq->bceskq/dot_general | solution.py:117
  39.1 2.4 %all-to-all-done = bf16[2,256,256]{2,0,1:T(2,128)(2,1)} async-done(((bf16[2,256,256]{2,0,1:T(2,128)(2,1)}), bf16[2,256,256]{2,0,1:T(2,128)(2,1)}, u32[]{:S(2)}, u32[]{:S(2)}) %all-to-all-start) | async-done | bytes 262176 | tf_op jit(solution)/shard_map/all_to_all | solution.py:99
  41.5 1.7 %convolution_bitcast_fusion = f32[2,32,2,2,8,256]{5,4,3,2,1,0:T(8,128)S(1)} fusion(f32[2,2,8,8,1,1]{3,2,1,0,5,4:T(8,128)S(1)} %copy-done.15, bf16[2,8,32,256]{3,0,2,1:T(2,128)(2,1)} %bitcast.18), kind=kOutput, calls=%fused_computation.14 | convolution fusion | flops 25165824 | bytes 2360320 | tf_op jit(solution)/shard_map/erkp,bcpm->bcerkm/dot_general | solution.py:115
  44.7 2.7 %fusion.10 = f32[2,32,2,2,8,256]{5,1,4,2,0,3:T(8,128)S(1)} fusion(f32[2,32,2,2,8,256]{5,4,3,2,1,0:T(8,128)S(1)} %pad_maximum_fusion, f32[1,256,2,256]{3,1,0,2:T(8,128)S(1)} %copy-done.4, f32[1,256,2,256]{3,1,0,2:T(8,128)S(1)} %copy-done.2), kind=kOutput, calls=%fused_computation.12 | convolution fusion | flops 1610874880 | bytes 5242880 | tf_op jit(solution)/shard_map/bcerkm,rmsq->bceskq/dot_general | solution.py:117
  48.1 2.7 %fusion.13 = f32[2,32,2,2,8,256]{5,4,3,2,1,0:T(8,128)S(1)} fusion(f32[2,32,2,2,8,256,1]{5,1,4,2,0,3,6:T(8,128)S(1)} %maximum_bitcast_fusion, f32[1,256,2,256]{3,1,0,2:T(8,128)S(1)} %copy-done.4, f32[1,256,2,256]{3,1,0,2:T(8,128)S(1)} %copy-done.2), kind=kOutput, calls=%fused_computation.13 | convolution fusion | flops 1610874880 | bytes 5242880 | tf_op jit(solution)/shard_map/bceskq,rmsq->bcerkm/dot_general | solution.py:122
  52.2 8.7 %all_to_all.39 = bf16[2,32,8,256]{3,1,0,2:T(8,128)(2,1)S(1)} all-to-all(bf16[2,32,8,256]{3,1,0,2:T(8,128)(2,1)S(1)} %copy.44), channel_id=1, replica_groups=mesh['seq'=8,'panel'=4] {'seq'}, dimensions={2} | all-to-all | bytes 524288 | tf_op jit(solution)/shard_map/all_to_all | solution.py:107
  61.8 1.2 %copy.46 = f32[2,256,256]{1,2,0:T(8,128)S(1)} copy(f32[2,256,256]{2,1,0:T(8,128)} %bitcast.214) | data formatting | bytes 1048576 | tf_op jit(solution)/shard_map/transpose | solution.py:110
  64.5 3.1 %collective-permute-start.10 = (f32[3,2,256]{2,1,0:T(2,128)S(1)}, f32[3,2,256]{2,1,0:T(2,128)S(1)}, u32[]{:S(2)}, u32[]{:S(2)}) collective-permute-start(f32[3,2,256]{2,1,0:T(2,128)S(1)} %slice.132), channel_id=1, source_target_pairs={{4,0},{8,4},{12,8},{16,12},{20,16},{24,20},{28,24},{5,1},{9,5},{13... | collective-permute-start | bytes 18440 | tf_op jit(solution)/shard_map/ppermute | solution.py:17
  67.9 2.7 %collective-permute-start.7 = (bf16[256,256]{1,0:T(8,128)(2,1)S(1)}, bf16[256,256]{1,0:T(8,128)(2,1)S(1)}, u32[]{:S(2)}, u32[]{:S(2)}) collective-permute-start(bf16[256,256]{1,0:T(8,128)(2,1)S(1)} %convolution_convert_fusion.2), channel_id=1, source_target_pairs={{0,1},{1,2},{2,3},{3,0},{4,5},{5,6},{6,7},{7,4},{8,9},{9,10},{10,1... | collective-permute-start | bytes 393224 | tf_op jit(solution)/shard_map/ppermute | solution.py:36
  72.8 1.2 %collective-permute-start.11 = (bf16[256,256]{1,0:T(8,128)(2,1)S(1)}, bf16[256,256]{1,0:T(8,128)(2,1)S(1)}, u32[]{:S(2)}, u32[]{:S(2)}) collective-permute-start(bf16[256,256]{1,0:T(8,128)(2,1)S(1)} %fusion.30), channel_id=1, source_target_pairs={{0,1},{1,2},{2,3},{3,0},{4,5},{5,6},{6,7},{7,4},{8,9},{9,10},{10,1... | collective-permute-start | bytes 393224 | tf_op jit(solution)/shard_map/ppermute | solution.py:36
  74.0 3.2 %collective-permute-start.12 = (bf16[256,256]{1,0:T(8,128)(2,1)S(1)}, bf16[256,256]{1,0:T(8,128)(2,1)S(1)}, u32[]{:S(2)}, u32[]{:S(2)}) collective-permute-start(bf16[256,256]{1,0:T(8,128)(2,1)S(1)} %fusion.31), channel_id=1, source_target_pairs={{0,2},{1,3},{2,0},{3,1},{4,6},{5,7},{6,4},{7,5},{8,10},{9,11},{10,... | collective-permute-start | bytes 393224 | tf_op jit(solution)/shard_map/ppermute | solution.py:36
  77.5 2.0 %collective-permute-done.7 = bf16[256,256]{1,0:T(8,128)(2,1)S(1)} collective-permute-done((bf16[256,256]{1,0:T(8,128)(2,1)S(1)}, bf16[256,256]{1,0:T(8,128)(2,1)S(1)}, u32[]{:S(2)}, u32[]{:S(2)}) %collective-permute-start.7) | collective-permute-done | bytes 131104 | tf_op jit(solution)/shard_map/ppermute | solution.py:36
  79.5 8.4 %collective-permute-done.8 = bf16[256,256]{1,0:T(8,128)(2,1)S(1)} collective-permute-done((bf16[256,256]{1,0:T(8,128)(2,1)S(1)}, bf16[256,256]{1,0:T(8,128)(2,1)S(1)}, u32[]{:S(2)}, u32[]{:S(2)}) %collective-permute-start.8) | collective-permute-done | bytes 131104 | tf_op jit(solution)/shard_map/ppermute | solution.py:36
  89.7 1.0 %collective-permute-done.11 = bf16[256,256]{1,0:T(8,128)(2,1)S(1)} collective-permute-done((bf16[256,256]{1,0:T(8,128)(2,1)S(1)}, bf16[256,256]{1,0:T(8,128)(2,1)S(1)}, u32[]{:S(2)}, u32[]{:S(2)}) %collective-permute-start.11) | collective-permute-done | bytes 131104 | tf_op jit(solution)/shard_map/ppermute | solution.py:36
  90.7 2.7 %collective-permute-done.12 = bf16[256,256]{1,0:T(8,128)(2,1)S(1)} collective-permute-done((bf16[256,256]{1,0:T(8,128)(2,1)S(1)}, bf16[256,256]{1,0:T(8,128)(2,1)S(1)}, u32[]{:S(2)}, u32[]{:S(2)}) %collective-permute-start.12) | collective-permute-done | bytes 131104 | tf_op jit(solution)/shard_map/ppermute | solution.py:36
  93.5 1.0 %collective-permute-done.13 = bf16[256,256]{1,0:T(8,128)(2,1)S(1)} collective-permute-done((bf16[256,256]{1,0:T(8,128)(2,1)S(1)}, bf16[256,256]{1,0:T(8,128)(2,1)S(1)}, u32[]{:S(2)}, u32[]{:S(2)}) %collective-permute-start.13) | collective-permute-done | bytes 131104 | tf_op jit(solution)/shard_map/ppermute | solution.py:36
  94.5 1.0 %fusion.62 = bf16[256,256]{1,0:T(8,128)(2,1)} fusion(bf16[3,256,256]{2,1,0:T(8,128)(2,1)S(1)} %fusion.39, bf16[3,1024,256]{2,1,0:T(8,128)(2,1)S(1)} %copy-done, s32[]{:T(128)S(6)} %select_n.85, bf16[256,256]{1,0:T(8,128)(2,1)S(1)} %collective-permute-done.13, bf16[256,256]{1,0:T(8,128)(2,1)S(1)} %collective-permute-done.12, ...), kind=kOutput, calls=%fused_computation.87 | convolution fusion | flops 101122048 | bytes 1310724 | tf_op jit(solution)/shard_map/jtc,jdc->td/dot_general | solution.py:210
  (88 shorter events, 17.2 us)
Async XLA Ops:
  0.6 17.6 %copy-start = (bf16[3,1024,256]{2,1,0:T(8,128)(2,1)S(1)}, bf16[3,1024,256]{2,1,0:T(8,128)(2,1)}, u32[]{:S(2)}) copy-start(bf16[3,1024,256]{2,1,0:T(8,128)(2,1)} %param.13) | copy-start | bytes 4718596
  0.6 17.6 %copy-start.11 = (bf16[256,256]{1,0:T(8,128)(2,1)S(1)}, bf16[256,256]{1,0:T(8,128)(2,1)}, u32[]{:S(2)}) copy-start(bf16[256,256]{1,0:T(8,128)(2,1)} %param.11) | copy-start | bytes 393220
  0.7 18.9 %collective-permute-start = (bf16[256,256]{1,0:T(8,128)(2,1)}, bf16[256,256]{1,0:T(8,128)(2,1)}, u32[]{:S(2)}, u32[]{:S(2)}) collective-permute-start(bf16[256,256]{1,0:T(8,128)(2,1)} %param.11), channel_id=1, source_target_pairs={{0,1},{1,2},{2,3},{3,0},{4,5},{5,6},{6,7},{7,4},{8,9},{9,10},{10,1... | collective-permute-start | bytes 393224 | tf_op jit(solution)/shard_map/ppermute | solution.py:25
  2.0 19.3 %collective-permute-start.2 = (bf16[256,256]{1,0:T(8,128)(2,1)}, bf16[256,256]{1,0:T(8,128)(2,1)}, u32[]{:S(2)}, u32[]{:S(2)}) collective-permute-start(bf16[256,256]{1,0:T(8,128)(2,1)} %param.11), channel_id=1, source_target_pairs={{0,3},{1,0},{2,1},{3,2},{4,7},{5,4},{6,5},{7,6},{8,11},{9,8},{10,9... | collective-permute-start | bytes 393224 | tf_op jit(solution)/shard_map/ppermute | solution.py:25
  2.2 20.4 %collective-permute-start.1 = (bf16[256,256]{1,0:T(8,128)(2,1)}, bf16[256,256]{1,0:T(8,128)(2,1)}, u32[]{:S(2)}, u32[]{:S(2)}) collective-permute-start(bf16[256,256]{1,0:T(8,128)(2,1)} %param.11), channel_id=1, source_target_pairs={{0,2},{1,3},{2,0},{3,1},{4,6},{5,7},{6,4},{7,5},{8,10},{9,11},{10,... | collective-permute-start | bytes 393224 | tf_op jit(solution)/shard_map/ppermute | solution.py:25
  4.5 23.1 %collective-permute-start.4 = (bf16[256,256]{1,0:T(8,128)(2,1)}, bf16[256,256]{1,0:T(8,128)(2,1)}, u32[]{:S(2)}, u32[]{:S(2)}) collective-permute-start(bf16[256,256]{1,0:T(8,128)(2,1)} %param.12), channel_id=1, source_target_pairs={{0,1},{1,2},{2,3},{3,0},{4,5},{5,6},{6,7},{7,4},{8,9},{9,10},{10,1... | collective-permute-start | bytes 393224 | tf_op jit(solution)/shard_map/ppermute | solution.py:25
  5.5 23.3 %collective-permute-start.6 = (bf16[256,256]{1,0:T(8,128)(2,1)}, bf16[256,256]{1,0:T(8,128)(2,1)}, u32[]{:S(2)}, u32[]{:S(2)}) collective-permute-start(bf16[256,256]{1,0:T(8,128)(2,1)} %param.12), channel_id=1, source_target_pairs={{0,3},{1,0},{2,1},{3,2},{4,7},{5,4},{6,5},{7,6},{8,11},{9,8},{10,9... | collective-permute-start | bytes 393224 | tf_op jit(solution)/shard_map/ppermute | solution.py:25
  7.7 24.2 %all-to-all-start.1 = ((f32[1,256,256]{2,0,1:T(1,128)}), f32[1,256,256]{2,0,1:T(1,128)S(1)}, u32[]{:S(2)}, u32[]{:S(2)}) async-start(f32[1,256,256]{2,0,1:T(1,128)} %bitcast.34), calls=%async_computation.1 | async-start | bytes 524288 | tf_op jit(solution)/shard_map/all_to_all | solution.py:99
  19.6 10.3 %collective-permute-start.5 = (bf16[256,256]{1,0:T(8,128)(2,1)}, bf16[256,256]{1,0:T(8,128)(2,1)S(1)}, u32[]{:S(2)}, u32[]{:S(2)}) collective-permute-start(bf16[256,256]{1,0:T(8,128)(2,1)} %param.12), channel_id=1, source_target_pairs={{0,2},{1,3},{2,0},{3,1},{4,6},{5,7},{6,4},{7,5},{8,10},{9,11},{10,... | collective-permute-start | bytes 393224 | tf_op jit(solution)/shard_map/ppermute | solution.py:25
  21.3 6.3 %copy-start.7 = (bf16[256,1024]{1,0:T(8,128)(2,1)S(1)}, bf16[256,1024]{1,0:T(8,128)(2,1)}, u32[]{:S(2)}) copy-start(bf16[256,1024]{1,0:T(8,128)(2,1)} %param.17) | copy-start | bytes 1572868
  21.3 6.3 %copy-start.9 = (f32[256,256]{0,1:T(8,128)S(1)}, f32[256,256]{0,1:T(8,128)}, u32[]{:S(2)}) copy-start(f32[256,256]{0,1:T(8,128)} %fusion.98) | copy-start | bytes 786436
  23.8 6.4 %collective-permute-start.3 = (bf16[3,2,256]{2,1,0:T(2,128)(2,1)S(1)}, bf16[3,2,256]{2,1,0:T(2,128)(2,1)S(1)}, u32[]{:S(2)}, u32[]{:S(2)}) collective-permute-start(bf16[3,2,256]{2,1,0:T(2,128)(2,1)S(1)} %slice.111), channel_id=1, source_target_pairs={{0,4},{4,8},{8,12},{12,16},{16,20},{20,24},{24,28},{1,5},{5,9},{9,... | collective-permute-start | bytes 9224 | tf_op jit(solution)/shard_map/ppermute | solution.py:17
  30.9 5.2 %copy-start.16 = (f32[2,2,8,8,1]{3,2,4,1,0:T(8,128)S(1)}, f32[2,2,8,8,1]{3,2,4,1,0:T(8,128)}, u32[]{:S(2)}) copy-start(f32[2,2,8,8,1]{3,2,4,1,0:T(8,128)} %constant.93) | copy-start | bytes 3076
  31.0 5.8 %copy-start.10 = (f32[2,8,256]{2,1,0:T(8,128)S(1)}, f32[2,8,256]{2,1,0:T(8,128)}, u32[]{:S(2)}) copy-start(f32[2,8,256]{2,1,0:T(8,128)} %constant.88.clone) | copy-start | bytes 49156
  31.0 5.8 %copy-start.12 = (f32[2,8,256]{2,1,0:T(8,128)S(1)}, f32[2,8,256]{2,1,0:T(8,128)}, u32[]{:S(2)}) copy-start(f32[2,8,256]{2,1,0:T(8,128)} %constant.89.clone) | copy-start | bytes 49156
  31.9 9.6 %all-to-all-start = ((bf16[2,256,256]{2,0,1:T(2,128)(2,1)}), bf16[2,256,256]{2,0,1:T(2,128)(2,1)}, u32[]{:S(2)}, u32[]{:S(2)}) async-start(bf16[2,256,256]{2,0,1:T(2,128)(2,1)} %copy.34), calls=%async_computation | async-start | bytes 524288 | tf_op jit(solution)/shard_map/all_to_all | solution.py:99
  36.7 1.0 %copy-start.1 = (f32[1,256,2,256]{3,1,0,2:T(8,128)S(1)}, f32[1,256,2,256]{3,1,0,2:T(8,128)}, u32[]{:S(2)}) copy-start(f32[1,256,2,256]{3,1,0,2:T(8,128)} %get-tuple-element.20) | copy-start | bytes 1572868
  36.7 1.2 %copy-start.3 = (f32[1,256,2,256]{3,1,0,2:T(8,128)S(1)}, f32[1,256,2,256]{3,1,0,2:T(8,128)}, u32[]{:S(2)}) copy-start(f32[1,256,2,256]{3,1,0,2:T(8,128)} %get-tuple-element.21) | copy-start | bytes 1572868
  37.9 3.5 %copy-start.15 = (f32[2,2,8,8,1,1]{3,2,1,0,5,4:T(8,128)S(1)}, f32[2,2,8,8,1,1]{3,2,1,0,5,4:T(8,128)}, u32[]{:S(2)}) copy-start(f32[2,2,8,8,1,1]{3,2,1,0,5,4:T(8,128)} %constant.92) | copy-start | bytes 3076
  43.5 1.0 %copy-start.2 = (f32[1,256,2,256]{3,1,0,2:T(8,128)S(1)}, f32[1,256,2,256]{3,1,0,2:T(8,128)}, u32[]{:S(2)}) copy-start(f32[1,256,2,256]{3,1,0,2:T(8,128)} %get-tuple-element.20) | copy-start | bytes 1572868
  43.5 1.2 %copy-start.4 = (f32[1,256,2,256]{3,1,0,2:T(8,128)S(1)}, f32[1,256,2,256]{3,1,0,2:T(8,128)}, u32[]{:S(2)}) copy-start(f32[1,256,2,256]{3,1,0,2:T(8,128)} %get-tuple-element.21) | copy-start | bytes 1572868
  48.0 2.7 %copy-start.14 = (f32[2,8,256]{2,1,0:T(8,128)S(1)}, f32[2,8,256]{2,1,0:T(8,128)}, u32[]{:S(2)}) copy-start(f32[2,8,256]{2,1,0:T(8,128)} %constant.91) | copy-start | bytes 49156
  51.5 11.5 %copy-start.6 = (f32[256,256]{1,0:T(8,128)S(1)}, f32[256,256]{1,0:T(8,128)}, u32[]{:S(2)}) copy-start(f32[256,256]{1,0:T(8,128)} %copy-done.5) | copy-start | bytes 786436
  51.5 11.5 %copy-start.17 = (f32[256]{0:T(256)S(1)}, f32[256]{0:T(256)}, u32[]{:S(2)}) copy-start(f32[256]{0:T(256)} %param.15) | copy-start | bytes 3076
  63.0 1.0 %copy-start.8 = (bf16[256,1024]{1,0:T(8,128)(2,1)S(1)}, bf16[256,1024]{1,0:T(8,128)(2,1)}, u32[]{:S(2)}) copy-start(bf16[256,1024]{1,0:T(8,128)(2,1)} %param.17) | copy-start | bytes 1572868
  64.5 7.3 %collective-permute-start.10 = (f32[3,2,256]{2,1,0:T(2,128)S(1)}, f32[3,2,256]{2,1,0:T(2,128)S(1)}, u32[]{:S(2)}, u32[]{:S(2)}) collective-permute-start(f32[3,2,256]{2,1,0:T(2,128)S(1)} %slice.132), channel_id=1, source_target_pairs={{4,0},{8,4},{12,8},{16,12},{20,16},{24,20},{28,24},{5,1},{9,5},{13... | collective-permute-start | bytes 18440 | tf_op jit(solution)/shard_map/ppermute | solution.py:17
  67.9 11.6 %collective-permute-start.7 = (bf16[256,256]{1,0:T(8,128)(2,1)S(1)}, bf16[256,256]{1,0:T(8,128)(2,1)S(1)}, u32[]{:S(2)}, u32[]{:S(2)}) collective-permute-start(bf16[256,256]{1,0:T(8,128)(2,1)S(1)} %convolution_convert_fusion.2), channel_id=1, source_target_pairs={{0,1},{1,2},{2,3},{3,0},{4,5},{5,6},{6,7},{7,4},{8,9},{9,10},{10,1... | collective-permute-start | bytes 393224 | tf_op jit(solution)/shard_map/ppermute | solution.py:36
  70.6 17.4 %collective-permute-start.8 = (bf16[256,256]{1,0:T(8,128)(2,1)S(1)}, bf16[256,256]{1,0:T(8,128)(2,1)S(1)}, u32[]{:S(2)}, u32[]{:S(2)}) collective-permute-start(bf16[256,256]{1,0:T(8,128)(2,1)S(1)} %convolution_convert_fusion.1), channel_id=1, source_target_pairs={{0,2},{1,3},{2,0},{3,1},{4,6},{5,7},{6,4},{7,5},{8,10},{9,11},{10,... | collective-permute-start | bytes 393224 | tf_op jit(solution)/shard_map/ppermute | solution.py:36
  71.5 17.3 %collective-permute-start.9 = (bf16[256,256]{1,0:T(8,128)(2,1)S(1)}, bf16[256,256]{1,0:T(8,128)(2,1)S(1)}, u32[]{:S(2)}, u32[]{:S(2)}) collective-permute-start(bf16[256,256]{1,0:T(8,128)(2,1)S(1)} %convolution_convert_fusion), channel_id=1, source_target_pairs={{0,3},{1,0},{2,1},{3,2},{4,7},{5,4},{6,5},{7,6},{8,11},{9,8},{10,9... | collective-permute-start | bytes 393224 | tf_op jit(solution)/shard_map/ppermute | solution.py:36
  72.8 17.9 %collective-permute-start.11 = (bf16[256,256]{1,0:T(8,128)(2,1)S(1)}, bf16[256,256]{1,0:T(8,128)(2,1)S(1)}, u32[]{:S(2)}, u32[]{:S(2)}) collective-permute-start(bf16[256,256]{1,0:T(8,128)(2,1)S(1)} %fusion.30), channel_id=1, source_target_pairs={{0,1},{1,2},{2,3},{3,0},{4,5},{5,6},{6,7},{7,4},{8,9},{9,10},{10,1... | collective-permute-start | bytes 393224 | tf_op jit(solution)/shard_map/ppermute | solution.py:36
  74.0 19.4 %collective-permute-start.12 = (bf16[256,256]{1,0:T(8,128)(2,1)S(1)}, bf16[256,256]{1,0:T(8,128)(2,1)S(1)}, u32[]{:S(2)}, u32[]{:S(2)}) collective-permute-start(bf16[256,256]{1,0:T(8,128)(2,1)S(1)} %fusion.31), channel_id=1, source_target_pairs={{0,2},{1,3},{2,0},{3,1},{4,6},{5,7},{6,4},{7,5},{8,10},{9,11},{10,... | collective-permute-start | bytes 393224 | tf_op jit(solution)/shard_map/ppermute | solution.py:36
  79.5 15.0 %collective-permute-start.13 = (bf16[256,256]{1,0:T(8,128)(2,1)S(1)}, bf16[256,256]{1,0:T(8,128)(2,1)S(1)}, u32[]{:S(2)}, u32[]{:S(2)}) collective-permute-start(bf16[256,256]{1,0:T(8,128)(2,1)S(1)} %fusion.32), channel_id=1, source_target_pairs={{0,3},{1,0},{2,1},{3,2},{4,7},{5,4},{6,5},{7,6},{8,11},{9,8},{10,9... | collective-permute-start | bytes 393224 | tf_op jit(solution)/shard_map/ppermute | solution.py:36
  (2 other events, 1.5 us)
where the time goes:
time: 96.3 us; the launch traced here: 95.5 us
  starting transfers between devices  31.1 us (32%)
  matrix products  21.1 us (22%)
  waiting for transfers between devices  18.5 us (19%)
  blocking collectives  8.7 us (9%)
  local copies, waits for them, and re-layouts  8.3 us (9%)
  other arithmetic  6.54 us (7%)
  between operations  1.23 us (1%)
    ppermute x6, waiting for transfers between devices, panel_reduce_scatter(): lax.ppermute(sent, 'panel', [(i, (i + k) % count) for i in range(count)])  16.1 us
    all_to_all x2, starting transfers between devices, to_columns(): lax.all_to_all(jnp.swapaxes(rows, 1, 2).astype(wire), 'seq', split_axis=1...  9.98 us
    all_to_all x1, blocking collectives, to_rows(): lax.all_to_all(columns.astype(wire), 'seq', split_axis=2, concat_axis=1,...  8.7 us
    ppermute x6, starting transfers between devices, panel_reduce_scatter(): lax.ppermute(sent, 'panel', [(i, (i + k) % count) for i in range(count)])  8.36 us
    ppermute x2, starting transfers between devices, shifted(): lax.ppermute(value, axis, [(source, source + steps) for source in range(i...  6.95 us
    ppermute x6, starting transfers between devices, panel_parts(): lax.ppermute(value, 'panel', [(i, (i + k) % count) for i in range(count)])  5.8 us
    dot_general x4, matrix products, local(): lax.dot_general(part, lax.dynamic_slice_in_dim(out_weight, source * width...  4.43 us
    dot_general x4, matrix products, local(): jnp.einsum('td,jdc->jtc', part, lax.dynamic_slice_in_dim(in_weight, sourc...  3.86 us
  transfers between devices with their start and end apart: 16, of which 7 were waited for; matrix products, arithmetic and copies ran while one was open for 20% of the time, Pallas kernels for 0%

commit v1 on v0

--- a/solution.py
+++ b/solution.py
@@ -9,6 +9,33 @@
 STAGE_A_PRECISION = lax.Precision.HIGH
 STAGE_B_PRECISION = lax.Precision.HIGH
 WIRE = jnp.bfloat16
+
+
+def find_cycles(slab_in, array_axis, local_array):
+    tmp, spare = (slab_in.shape[:array_axis], slab_in.shape[array_axis + 1 :])
+    next_value = slab_in.reshape(*tmp, local_array, -1, *spare)
+    return jnp.moveaxis(next_value, array_axis, 0)
+
+
+def _test_lots_all(s0, axis_no):
+    s0 = jnp.moveaxis(s0, 0, axis_no)
+    carry = s0.shape
+    return s0.reshape(*carry[:axis_no], carry[axis_no] * carry[axis_no + 1], *carry[axis_no + 2 :])
+
+
+def _make_sheets(t0, device_axis, field, base_x):
+    arr_out = lax.axis_size(device_axis)
+    arr_next = lax.axis_index(device_axis)
+    ready, a_next = (arr_out, arr_next)
+    carry_out = find_cycles(t0, field, ready)
+    bank = [carry_out[a_next]]
+    for dev in range(1, ready):
+        answer = carry_out[a_next ^ dev]
+        mixed_arr = lax.ppermute(answer, device_axis, perm=[(k0, k0 ^ dev) for k0 in range(ready)])
+        bank.append(mixed_arr)
+    r2 = jnp.stack(bank, 0)
+    carry_out = r2[a_next ^ jnp.arange(ready)]
+    return _test_lots_all(carry_out, base_x)
 
 
 def shifted(value, axis, steps):
@@ -96,9 +123,7 @@
 def to_columns(rows, wire=jnp.float32):
     shard_count = lax.axis_size("seq")
     batch, row_count, _ = rows.shape
-    columns = lax.all_to_all(
-        jnp.swapaxes(rows, 1, 2).astype(wire), "seq", split_axis=1, concat_axis=2, tiled=True
-    ).astype(jnp.float32)
+    columns = _make_sheets(jnp.swapaxes(rows, 1, 2).astype(wire), "seq", 1, 2).astype(jnp.float32)
     return columns.reshape(batch, columns.shape[1], shard_count, row_count)
 
 

time: 96.3 us -> 133 us (1.38)
  starting transfers between devices: 31.1 us -> 43.6 us
  local copies, waits for them, and re-layouts: 8.3 us -> 19 us
  waiting for transfers between devices: 18.5 us -> 29.2 us
  other arithmetic: 6.54 us -> 8.48 us
    ppermute x0 -> x14, starting transfers between devices: none -> 22 us  [_make_sheets(): lax.ppermute(answer, device_axis, perm=[(k0, k0 ^ dev) for k0 in range(re...]
    ppermute x0 -> x14, waiting for transfers between devices: none -> 13.2 us  [_make_sheets(): lax.ppermute(answer, device_axis, perm=[(k0, k0 ^ dev) for k0 in range(re...]
    all_to_all x2 -> x0, starting transfers between devices: 9.98 us -> none  [to_columns(): lax.all_to_all(jnp.swapaxes(rows, 1, 2).astype(wire), 'seq', split_axis=1...]
    unnamed x37 -> x68, local copies, waits for them, and re-layouts: 3.63 us -> 10.2 us
    gather x0 -> x2, local copies, waits for them, and re-layouts: none -> 2.91 us  [_make_sheets(): carry_out = r2[a_next ^ jnp.arange(ready)]]
    all_to_all x2 -> x0, waiting for transfers between devices: 2.4 us -> none  [to_columns(): lax.all_to_all(jnp.swapaxes(rows, 1, 2).astype(wire), 'seq', split_axis=1...]
    broadcast_in_dim x1 -> x0, local copies, waits for them, and re-layouts: 1.79 us -> none  [local(): filt_spec = forward_spectrum(to_columns(long_filter[None]), tables)]
  transfers between devices with their start and end apart: 16 -> 28, of which waited for: 7 -> 14; matrix products, arithmetic and copies ran while one was open for 20% -> 20% of each run, Pallas kernels for 0% -> 0%
where the time goes in v1:
time: 133 us; the launch traced here: 132 us
  starting transfers between devices  43.6 us (33%)
  waiting for transfers between devices  29.2 us (22%)
  matrix products  21.4 us (16%)
  local copies, waits for them, and re-layouts  19 us (14%)
  blocking collectives  8.76 us (7%)
  other arithmetic  8.48 us (6%)
  between operations  1.38 us (1%)
    ppermute x14, starting transfers between devices, _make_sheets(): lax.ppermute(answer, device_axis, perm=[(k0, k0 ^ dev) for k0 in range(re...  22 us
    ppermute x6, waiting for transfers between devices, panel_reduce_scatter(): lax.ppermute(sent, 'panel', [(i, (i + k) % count) for i in range(count)])  16 us
    ppermute x14, waiting for transfers between devices, _make_sheets(): lax.ppermute(answer, device_axis, perm=[(k0, k0 ^ dev) for k0 in range(re...  13.2 us
    unnamed x68, local copies, waits for them, and re-layouts  10.2 us
    all_to_all x1, blocking collectives, to_rows(): lax.all_to_all(columns.astype(wire), 'seq', split_axis=2, concat_axis=1,...  8.76 us
    ppermute x6, starting transfers between devices, panel_reduce_scatter(): lax.ppermute(sent, 'panel', [(i, (i + k) % count) for i in range(count)])  8.35 us
    ppermute x2, starting transfers between devices, shifted(): lax.ppermute(value, axis, [(source, source + steps) for source in range(i...  7.48 us
    ppermute x6, starting transfers between devices, panel_parts(): lax.ppermute(value, 'panel', [(i, (i + k) % count) for i in range(count)])  5.84 us
  transfers between devices with their start and end apart: 28, of which 14 were waited for; matrix products, arithmetic and copies ran while one was open for 20% of the time, Pallas kernels for 0%

profile of v1, /device:TPU:9, one launch (start us, length us, event | category | flops | bytes accessed | tf_op | source)
XLA Modules:
  0.0 131.9 jit_solution(10498507975092859598)
XLA Ops:
  2.2 2.3 %collective-permute-start.1 = (bf16[256,256]{1,0:T(8,128)(2,1)}, bf16[256,256]{1,0:T(8,128)(2,1)}, u32[]{:S(2)}, u32[]{:S(2)}) collective-permute-start(bf16[256,256]{1,0:T(8,128)(2,1)} %param.11), channel_id=1, source_target_pairs={{0,2},{1,3},{2,0},{3,1},{4,6},{5,7},{6,4},{7,5},{8,10},{9,11},{10,... | collective-permute-start | bytes 393224 | tf_op jit(solution)/shard_map/ppermute | solution.py:52
  6.6 1.6 %collective-permute-start.14 = (f32[1,32,256]{2,1,0:T(8,128)S(1)}, f32[1,32,256]{2,1,0:T(8,128)}, u32[]{:S(2)}, u32[]{:S(2)}) collective-permute-start(f32[1,32,256]{2,1,0:T(8,128)S(1)} %get-tuple-element.26), channel_id=1, source_target_pairs={{0,4},{4,0},{8,12},{12,8},{16,20},{20,16},{24,28},{28,24},{1,5},{5... | collective-permute-start | bytes 98312 | tf_op jit(solution)/shard_map/ppermute | solution.py:34
  12.1 1.9 %fusion.96 = f32[256,256]{0,1:T(8,128)} fusion(bf16[256,256]{1,0:T(8,128)(2,1)} %param.12, bf16[256,1024]{1,0:T(8,128)(2,1)} %param.17, s32[]{:T(128)S(6)} %select_n.128), kind=kOutput, calls=%fused_computation.134 | convolution fusion | flops 33554432 | bytes 524292 | tf_op jit(solution)/shard_map/dot_general | solution.py:169
  16.9 1.4 %collective-permute-start.15 = (f32[1,32,256]{2,1,0:T(8,128)S(1)}, f32[1,32,256]{2,1,0:T(8,128)S(1)}, u32[]{:S(2)}, u32[]{:S(2)}) collective-permute-start(f32[1,32,256]{2,1,0:T(8,128)S(1)} %get-tuple-element.25), channel_id=1, source_target_pairs={{0,8},{4,12},{8,0},{12,4},{16,24},{20,28},{24,16},{28,20},{1,9},{5... | collective-permute-start | bytes 98312 | tf_op jit(solution)/shard_map/ppermute | solution.py:34
  19.7 2.4 %collective-permute-start.16 = (f32[1,32,256]{2,1,0:T(8,128)S(1)}, f32[1,32,256]{2,1,0:T(8,128)S(1)}, u32[]{:S(2)}, u32[]{:S(2)}) collective-permute-start(f32[1,32,256]{2,1,0:T(8,128)S(1)} %get-tuple-element.24), channel_id=1, source_target_pairs={{0,12},{4,8},{8,4},{12,0},{16,28},{20,24},{24,20},{28,16},{1,13},{... | collective-permute-start | bytes 98312 | tf_op jit(solution)/shard_map/ppermute | solution.py:34
  22.1 1.8 %collective-permute-done.16 = f32[1,32,256]{2,1,0:T(8,128)S(1)} collective-permute-done((f32[1,32,256]{2,1,0:T(8,128)S(1)}, f32[1,32,256]{2,1,0:T(8,128)S(1)}, u32[]{:S(2)}, u32[]{:S(2)}) %collective-permute-start.16) | collective-permute-done | bytes 32800 | tf_op jit(solution)/shard_map/ppermute | solution.py:34
  24.0 1.6 %collective-permute-start.17 = (f32[1,32,256]{2,1,0:T(8,128)S(1)}, f32[1,32,256]{2,1,0:T(8,128)S(1)}, u32[]{:S(2)}, u32[]{:S(2)}) collective-permute-start(f32[1,32,256]{2,1,0:T(8,128)S(1)} %get-tuple-element.23), channel_id=1, source_target_pairs={{0,16},{4,20},{8,24},{12,28},{16,0},{20,4},{24,8},{28,12},{1,17},{... | collective-permute-start | bytes 98312 | tf_op jit(solution)/shard_map/ppermute | solution.py:34
  26.8 2.9 %collective-permute-start.18 = (f32[1,32,256]{2,1,0:T(8,128)S(1)}, f32[1,32,256]{2,1,0:T(8,128)S(1)}, u32[]{:S(2)}, u32[]{:S(2)}) collective-permute-start(f32[1,32,256]{2,1,0:T(8,128)S(1)} %get-tuple-element.22), channel_id=1, source_target_pairs={{0,20},{4,16},{8,28},{12,24},{16,4},{20,0},{24,12},{28,8},{1,21},{... | collective-permute-start | bytes 98312 | tf_op jit(solution)/shard_map/ppermute | solution.py:34
  29.7 1.6 %collective-permute-done.18 = f32[1,32,256]{2,1,0:T(8,128)S(1)} collective-permute-done((f32[1,32,256]{2,1,0:T(8,128)S(1)}, f32[1,32,256]{2,1,0:T(8,128)S(1)}, u32[]{:S(2)}, u32[]{:S(2)}) %collective-permute-start.18) | collective-permute-done | bytes 32800 | tf_op jit(solution)/shard_map/ppermute | solution.py:34
  32.2 2.8 %collective-permute-done.19 = f32[1,32,256]{2,1,0:T(8,128)S(1)} collective-permute-done((f32[1,32,256]{2,1,0:T(8,128)S(1)}, f32[1,32,256]{2,1,0:T(8,128)S(1)}, u32[]{:S(2)}, u32[]{:S(2)}) %collective-permute-start.19) | collective-permute-done | bytes 32800 | tf_op jit(solution)/shard_map/ppermute | solution.py:34
  35.0 3.5 %collective-permute-start.20 = (f32[1,32,256]{2,1,0:T(8,128)S(1)}, f32[1,32,256]{2,1,0:T(8,128)S(1)}, u32[]{:S(2)}, u32[]{:S(2)}) collective-permute-start(f32[1,32,256]{2,1,0:T(8,128)S(1)} %get-tuple-element.20), channel_id=1, source_target_pairs={{0,28},{4,24},{8,20},{12,16},{16,12},{20,8},{24,4},{28,0},{1,29},{... | collective-permute-start | bytes 98312 | tf_op jit(solution)/shard_map/ppermute | solution.py:34
  38.5 2.0 %collective-permute-done.20 = f32[1,32,256]{2,1,0:T(8,128)S(1)} collective-permute-done((f32[1,32,256]{2,1,0:T(8,128)S(1)}, f32[1,32,256]{2,1,0:T(8,128)S(1)}, u32[]{:S(2)}, u32[]{:S(2)}) %collective-permute-start.20) | collective-permute-done | bytes 32800 | tf_op jit(solution)/shard_map/ppermute | solution.py:34
  42.9 1.4 %convolution_bitcast_fusion.1 = f32[1,32,2,2,8,256]{5,1,4,2,0,3:T(8,128)S(1)} fusion(f32[32,2,2,8,256]{4,3,2,1,0:T(8,128)S(1)} %maximum_bitcast_fusion.1, f32[1,256,2,256]{3,1,0,2:T(8,128)S(1)} %copy-done.3, f32[1,256,2,256]{3,1,0,2:T(8,128)S(1)} %get-tuple-element.28), kind=kOutput, calls=%fused_computation.17 | convolution fusion | flops 805568512 | bytes 3145728 | tf_op jit(solution)/shard_map/bcerkm,rmsq->bceskq/dot_general | solution.py:142
  49.0 4.3 %collective-permute-start.3 = (bf16[3,2,256]{2,1,0:T(2,128)(2,1)S(1)}, bf16[3,2,256]{2,1,0:T(2,128)(2,1)S(1)}, u32[]{:S(2)}, u32[]{:S(2)}) collective-permute-start(bf16[3,2,256]{2,1,0:T(2,128)(2,1)S(1)} %slice.115), channel_id=1, source_target_pairs={{0,4},{4,8},{8,12},{12,16},{16,20},{20,24},{24,28},{1,5},{5,9},{9,... | collective-permute-start | bytes 9224 | tf_op jit(solution)/shard_map/ppermute | solution.py:44
  56.5 1.8 %copy.33 = bf16[2,256,256]{2,1,0:T(8,128)(2,1)} copy(bf16[2,256,256]{1,2,0:T(8,128)(2,1)} %maximum_bitcast_fusion.4) | data formatting | bytes 524288 | tf_op jit(solution)/shard_map/convert_element_type | solution.py:126
  59.2 1.4 %constant_dynamic-update-slice_fusion.7 = bf16[8,2,32,256]{3,2,1,0:T(8,128)(2,1)} fusion(bf16[2,8,32,256]{3,2,1,0:T(8,128)(2,1)} %bitcast.271, s32[]{:T(128)S(6)} %select_n.135), kind=kLoop, calls=%fused_computation.143 | loop fusion | bytes 65540
  60.6 1.5 %collective-permute-start.13 = (bf16[2,32,256]{2,1,0:T(8,128)(2,1)S(1)}, bf16[2,32,256]{2,1,0:T(8,128)(2,1)S(1)}, u32[]{:S(2)}, u32[]{:S(2)}) collective-permute-start(bf16[2,32,256]{2,1,0:T(8,128)(2,1)S(1)} %get-tuple-element.30), channel_id=1, source_target_pairs={{0,28},{4,24},{8,20},{12,16},{16,12},{20,8},{24,4},{28,0},{1,29},{... | collective-permute-start | bytes 98312 | tf_op jit(solution)/shard_map/ppermute | solution.py:34
  63.4 2.1 %collective-permute-start.11 = (bf16[2,32,256]{2,1,0:T(8,128)(2,1)S(1)}, bf16[2,32,256]{2,1,0:T(8,128)(2,1)S(1)}, u32[]{:S(2)}, u32[]{:S(2)}) collective-permute-start(bf16[2,32,256]{2,1,0:T(8,128)(2,1)S(1)} %get-tuple-element.32), channel_id=1, source_target_pairs={{0,20},{4,16},{8,28},{12,24},{16,4},{20,0},{24,12},{28,8},{1,21},{... | collective-permute-start | bytes 98312 | tf_op jit(solution)/shard_map/ppermute | solution.py:34
  66.9 1.7 %collective-permute-done.8 = bf16[2,32,256]{2,1,0:T(8,128)(2,1)S(1)} collective-permute-done((bf16[2,32,256]{2,1,0:T(8,128)(2,1)S(1)}, bf16[2,32,256]{2,1,0:T(8,128)(2,1)S(1)}, u32[]{:S(2)}, u32[]{:S(2)}) %collective-permute-start.8) | collective-permute-done | bytes 32800 | tf_op jit(solution)/shard_map/ppermute | solution.py:34
  68.5 2.0 %collective-permute-start.9 = (bf16[2,32,256]{2,1,0:T(8,128)(2,1)S(1)}, bf16[2,32,256]{2,1,0:T(8,128)(2,1)S(1)}, u32[]{:S(2)}, u32[]{:S(2)}) collective-permute-start(bf16[2,32,256]{2,1,0:T(8,128)(2,1)S(1)} %get-tuple-element.34), channel_id=1, source_target_pairs={{0,12},{4,8},{8,4},{12,0},{16,28},{20,24},{24,20},{28,16},{1,13},{... | collective-permute-start | bytes 98312 | tf_op jit(solution)/shard_map/ppermute | solution.py:34
  71.1 1.4 %collective-permute-done.9 = bf16[2,32,256]{2,1,0:T(8,128)(2,1)S(1)} collective-permute-done((bf16[2,32,256]{2,1,0:T(8,128)(2,1)S(1)}, bf16[2,32,256]{2,1,0:T(8,128)(2,1)S(1)}, u32[]{:S(2)}, u32[]{:S(2)}) %collective-permute-start.9) | collective-permute-done | bytes 32800 | tf_op jit(solution)/shard_map/ppermute | solution.py:34
  75.5 2.4 %gather_fusion = bf16[8,2,32,256]{3,2,1,0:T(8,128)(2,1)} fusion(bf16[8,2,32,256]{3,2,1,0:T(8,128)(2,1)} %constant_dynamic-update-slice_fusion, s32[1024]{0:T(1024)} %copy-done.25), kind=kCustom, calls=%fused_computation | custom fusion | bytes 524320 | tf_op jit(solution)/shard_map/gather | solution.py:37
  77.9 1.6 %convolution_bitcast_fusion = f32[2,32,2,2,8,256]{5,4,3,2,1,0:T(8,128)S(1)} fusion(f32[2,2,8,8,1,1]{3,2,1,0,5,4:T(8,128)S(1)} %copy-done.23, bf16[2,32,8,256,1,1]{3,1,0,2,5,4:T(8,128)(2,1)} %bitcast.268), kind=kOutput, calls=%fused_computation.16 | convolution fusion | flops 25165824 | bytes 2360320 | tf_op jit(solution)/shard_map/erkp,bcpm->bcerkm/dot_general | solution.py:140
  81.1 2.7 %fusion.10 = f32[2,32,2,2,8,256]{5,1,4,2,0,3:T(8,128)S(1)} fusion(f32[2,32,2,2,8,256]{5,4,3,2,1,0:T(8,128)S(1)} %pad_maximum_fusion, f32[1,256,2,256]{3,1,0,2:T(8,128)S(1)} %copy-done.4, f32[1,256,2,256]{3,1,0,2:T(8,128)S(1)} %copy-done.2), kind=kOutput, calls=%fused_computation.14 | convolution fusion | flops 1610874880 | bytes 5242880 | tf_op jit(solution)/shard_map/bcerkm,rmsq->bceskq/dot_general | solution.py:142
  84.4 2.7 %fusion.13 = f32[2,32,2,2,8,256]{5,4,3,2,1,0:T(8,128)S(1)} fusion(f32[2,32,2,2,8,256,1]{5,1,4,2,0,3,6:T(8,128)S(1)} %maximum_bitcast_fusion, f32[1,256,2,256]{3,1,0,2:T(8,128)S(1)} %copy-done.4, f32[1,256,2,256]{3,1,0,2:T(8,128)S(1)} %copy-done.2), kind=kOutput, calls=%fused_computation.15 | convolution fusion | flops 1610874880 | bytes 5242880 | tf_op jit(solution)/shard_map/bceskq,rmsq->bcerkm/dot_general | solution.py:147
  88.6 8.8 %all_to_all.4 = bf16[2,32,8,256]{3,1,0,2:T(8,128)(2,1)S(1)} all-to-all(bf16[2,32,8,256]{3,1,0,2:T(8,128)(2,1)S(1)} %copy.42), channel_id=1, replica_groups=mesh['seq'=8,'panel'=4] {'seq'}, dimensions={2} | all-to-all | bytes 524288 | tf_op jit(solution)/shard_map/all_to_all | solution.py:132
  101.0 3.1 %collective-permute-start.24 = (f32[3,2,256]{2,1,0:T(2,128)S(1)}, f32[3,2,256]{2,1,0:T(2,128)S(1)}, u32[]{:S(2)}, u32[]{:S(2)}) collective-permute-start(f32[3,2,256]{2,1,0:T(2,128)S(1)} %slice.136), channel_id=1, source_target_pairs={{4,0},{8,4},{12,8},{16,12},{20,16},{24,20},{28,24},{5,1},{9,5},{13... | collective-permute-start | bytes 18440 | tf_op jit(solution)/shard_map/ppermute | solution.py:44
  104.3 2.7 %collective-permute-start.21 = (bf16[256,256]{1,0:T(8,128)(2,1)S(1)}, bf16[256,256]{1,0:T(8,128)(2,1)S(1)}, u32[]{:S(2)}, u32[]{:S(2)}) collective-permute-start(bf16[256,256]{1,0:T(8,128)(2,1)S(1)} %convolution_convert_fusion.2), channel_id=1, source_target_pairs={{0,1},{1,2},{2,3},{3,0},{4,5},{5,6},{6,7},{7,4},{8,9},{9,10},{10,1... | collective-permute-start | bytes 393224 | tf_op jit(solution)/shard_map/ppermute | solution.py:63
  110.5 3.2 %collective-permute-start.26 = (bf16[256,256]{1,0:T(8,128)(2,1)S(1)}, bf16[256,256]{1,0:T(8,128)(2,1)S(1)}, u32[]{:S(2)}, u32[]{:S(2)}) collective-permute-start(bf16[256,256]{1,0:T(8,128)(2,1)S(1)} %fusion.31), channel_id=1, source_target_pairs={{0,2},{1,3},{2,0},{3,1},{4,6},{5,7},{6,4},{7,5},{8,10},{9,11},{10,... | collective-permute-start | bytes 393224 | tf_op jit(solution)/shard_map/ppermute | solution.py:63
  114.0 1.9 %collective-permute-done.21 = bf16[256,256]{1,0:T(8,128)(2,1)S(1)} collective-permute-done((bf16[256,256]{1,0:T(8,128)(2,1)S(1)}, bf16[256,256]{1,0:T(8,128)(2,1)S(1)}, u32[]{:S(2)}, u32[]{:S(2)}) %collective-permute-start.21) | collective-permute-done | bytes 131104 | tf_op jit(solution)/shard_map/ppermute | solution.py:63
  116.0 8.4 %collective-permute-done.22 = bf16[256,256]{1,0:T(8,128)(2,1)S(1)} collective-permute-done((bf16[256,256]{1,0:T(8,128)(2,1)S(1)}, bf16[256,256]{1,0:T(8,128)(2,1)S(1)}, u32[]{:S(2)}, u32[]{:S(2)}) %collective-permute-start.22) | collective-permute-done | bytes 131104 | tf_op jit(solution)/shard_map/ppermute | solution.py:63
  127.2 2.7 %collective-permute-done.26 = bf16[256,256]{1,0:T(8,128)(2,1)S(1)} collective-permute-done((bf16[256,256]{1,0:T(8,128)(2,1)S(1)}, bf16[256,256]{1,0:T(8,128)(2,1)S(1)}, u32[]{:S(2)}, u32[]{:S(2)}) %collective-permute-start.26) | collective-permute-done | bytes 131104 | tf_op jit(solution)/shard_map/ppermute | solution.py:63
  (150 shorter events, 46.8 us)
Async XLA Ops:
  0.7 43.7 %collective-permute-start = (bf16[256,256]{1,0:T(8,128)(2,1)}, bf16[256,256]{1,0:T(8,128)(2,1)}, u32[]{:S(2)}, u32[]{:S(2)}) collective-permute-start(bf16[256,256]{1,0:T(8,128)(2,1)} %param.11), channel_id=1, source_target_pairs={{0,1},{1,2},{2,3},{3,0},{4,5},{5,6},{6,7},{7,4},{8,9},{9,10},{10,1... | collective-permute-start | bytes 393224 | tf_op jit(solution)/shard_map/ppermute | solution.py:52
  2.0 44.4 %collective-permute-start.2 = (bf16[256,256]{1,0:T(8,128)(2,1)}, bf16[256,256]{1,0:T(8,128)(2,1)}, u32[]{:S(2)}, u32[]{:S(2)}) collective-permute-start(bf16[256,256]{1,0:T(8,128)(2,1)} %param.11), channel_id=1, source_target_pairs={{0,3},{1,0},{2,1},{3,2},{4,7},{5,4},{6,5},{7,6},{8,11},{9,8},{10,9... | collective-permute-start | bytes 393224 | tf_op jit(solution)/shard_map/ppermute | solution.py:52
  2.2 45.5 %collective-permute-start.1 = (bf16[256,256]{1,0:T(8,128)(2,1)}, bf16[256,256]{1,0:T(8,128)(2,1)}, u32[]{:S(2)}, u32[]{:S(2)}) collective-permute-start(bf16[256,256]{1,0:T(8,128)(2,1)} %param.11), channel_id=1, source_target_pairs={{0,2},{1,3},{2,0},{3,1},{4,6},{5,7},{6,4},{7,5},{8,10},{9,11},{10,... | collective-permute-start | bytes 393224 | tf_op jit(solution)/shard_map/ppermute | solution.py:52
  4.5 48.8 %collective-permute-start.4 = (bf16[256,256]{1,0:T(8,128)(2,1)}, bf16[256,256]{1,0:T(8,128)(2,1)}, u32[]{:S(2)}, u32[]{:S(2)}) collective-permute-start(bf16[256,256]{1,0:T(8,128)(2,1)} %param.12), channel_id=1, source_target_pairs={{0,1},{1,2},{2,3},{3,0},{4,5},{5,6},{6,7},{7,4},{8,9},{9,10},{10,1... | collective-permute-start | bytes 393224 | tf_op jit(solution)/shard_map/ppermute | solution.py:52
  6.6 10.2 %collective-permute-start.14 = (f32[1,32,256]{2,1,0:T(8,128)S(1)}, f32[1,32,256]{2,1,0:T(8,128)}, u32[]{:S(2)}, u32[]{:S(2)}) collective-permute-start(f32[1,32,256]{2,1,0:T(8,128)S(1)} %get-tuple-element.26), channel_id=1, source_target_pairs={{0,4},{4,0},{8,12},{12,8},{16,20},{20,16},{24,28},{28,24},{1,5},{5... | collective-permute-start | bytes 98312 | tf_op jit(solution)/shard_map/ppermute | solution.py:34
  14.1 27.2 %copy-start.24 = (f32[2,2,8,8,1]{3,2,1,0,4:T(8,128)S(1)}, f32[2,2,8,8,1]{3,2,1,0,4:T(8,128)}, u32[]{:S(2)}) copy-start(f32[2,2,8,8,1]{3,2,1,0,4:T(8,128)} %constant.108) | copy-start | bytes 3076
  15.3 26.6 %copy-start.11 = (f32[2,8,256]{2,1,0:T(8,128)S(1)}, f32[2,8,256]{2,1,0:T(8,128)}, u32[]{:S(2)}) copy-start(f32[2,8,256]{2,1,0:T(8,128)} %constant.103.clone) | copy-start | bytes 49156
  15.3 26.6 %copy-start.13 = (f32[2,8,256]{2,1,0:T(8,128)S(1)}, f32[2,8,256]{2,1,0:T(8,128)}, u32[]{:S(2)}) copy-start(f32[2,8,256]{2,1,0:T(8,128)} %constant.104.clone) | copy-start | bytes 49156
  16.2 26.0 %copy-start.1 = (f32[1,256,2,256]{3,1,0,2:T(8,128)}, f32[1,256,2,256]{3,1,0,2:T(8,128)S(1)}, u32[]{:S(2)}) copy-start(f32[1,256,2,256]{3,1,0,2:T(8,128)S(1)} %get-tuple-element.28) | copy-start | bytes 1572868
  16.9 2.8 %collective-permute-start.15 = (f32[1,32,256]{2,1,0:T(8,128)S(1)}, f32[1,32,256]{2,1,0:T(8,128)S(1)}, u32[]{:S(2)}, u32[]{:S(2)}) collective-permute-start(f32[1,32,256]{2,1,0:T(8,128)S(1)} %get-tuple-element.25), channel_id=1, source_target_pairs={{0,8},{4,12},{8,0},{12,4},{16,24},{20,28},{24,16},{28,20},{1,9},{5... | collective-permute-start | bytes 98312 | tf_op jit(solution)/shard_map/ppermute | solution.py:34
  19.7 4.3 %collective-permute-start.16 = (f32[1,32,256]{2,1,0:T(8,128)S(1)}, f32[1,32,256]{2,1,0:T(8,128)S(1)}, u32[]{:S(2)}, u32[]{:S(2)}) collective-permute-start(f32[1,32,256]{2,1,0:T(8,128)S(1)} %get-tuple-element.24), channel_id=1, source_target_pairs={{0,12},{4,8},{8,4},{12,0},{16,28},{20,24},{24,20},{28,16},{1,13},{... | collective-permute-start | bytes 98312 | tf_op jit(solution)/shard_map/ppermute | solution.py:34
  24.0 2.9 %collective-permute-start.17 = (f32[1,32,256]{2,1,0:T(8,128)S(1)}, f32[1,32,256]{2,1,0:T(8,128)S(1)}, u32[]{:S(2)}, u32[]{:S(2)}) collective-permute-start(f32[1,32,256]{2,1,0:T(8,128)S(1)} %get-tuple-element.23), channel_id=1, source_target_pairs={{0,16},{4,20},{8,24},{12,28},{16,0},{20,4},{24,8},{28,12},{1,17},{... | collective-permute-start | bytes 98312 | tf_op jit(solution)/shard_map/ppermute | solution.py:34
  26.8 4.5 %collective-permute-start.18 = (f32[1,32,256]{2,1,0:T(8,128)S(1)}, f32[1,32,256]{2,1,0:T(8,128)S(1)}, u32[]{:S(2)}, u32[]{:S(2)}) collective-permute-start(f32[1,32,256]{2,1,0:T(8,128)S(1)} %get-tuple-element.22), channel_id=1, source_target_pairs={{0,20},{4,16},{8,28},{12,24},{16,4},{20,0},{24,12},{28,8},{1,21},{... | collective-permute-start | bytes 98312 | tf_op jit(solution)/shard_map/ppermute | solution.py:34
  31.3 3.7 %collective-permute-start.19 = (f32[1,32,256]{2,1,0:T(8,128)S(1)}, f32[1,32,256]{2,1,0:T(8,128)S(1)}, u32[]{:S(2)}, u32[]{:S(2)}) collective-permute-start(f32[1,32,256]{2,1,0:T(8,128)S(1)} %get-tuple-element.21), channel_id=1, source_target_pairs={{0,24},{4,28},{8,16},{12,20},{16,8},{20,12},{24,0},{28,4},{1,25},{... | collective-permute-start | bytes 98312 | tf_op jit(solution)/shard_map/ppermute | solution.py:34
  35.0 5.5 %collective-permute-start.20 = (f32[1,32,256]{2,1,0:T(8,128)S(1)}, f32[1,32,256]{2,1,0:T(8,128)S(1)}, u32[]{:S(2)}, u32[]{:S(2)}) collective-permute-start(f32[1,32,256]{2,1,0:T(8,128)S(1)} %get-tuple-element.20), channel_id=1, source_target_pairs={{0,28},{4,24},{8,20},{12,16},{16,12},{20,8},{24,4},{28,0},{1,29},{... | collective-permute-start | bytes 98312 | tf_op jit(solution)/shard_map/ppermute | solution.py:34
  40.5 14.0 %collective-permute-start.6 = (bf16[256,256]{1,0:T(8,128)(2,1)}, bf16[256,256]{1,0:T(8,128)(2,1)S(1)}, u32[]{:S(2)}, u32[]{:S(2)}) collective-permute-start(bf16[256,256]{1,0:T(8,128)(2,1)} %param.12), channel_id=1, source_target_pairs={{0,3},{1,0},{2,1},{3,2},{4,7},{5,4},{6,5},{7,6},{8,11},{9,8},{10,9... | collective-permute-start | bytes 393224 | tf_op jit(solution)/shard_map/ppermute | solution.py:52
  44.4 10.3 %collective-permute-start.5 = (bf16[256,256]{1,0:T(8,128)(2,1)}, bf16[256,256]{1,0:T(8,128)(2,1)S(1)}, u32[]{:S(2)}, u32[]{:S(2)}) collective-permute-start(bf16[256,256]{1,0:T(8,128)(2,1)} %param.12), channel_id=1, source_target_pairs={{0,2},{1,3},{2,0},{3,1},{4,6},{5,7},{6,4},{7,5},{8,10},{9,11},{10,... | collective-permute-start | bytes 393224 | tf_op jit(solution)/shard_map/ppermute | solution.py:52
  49.0 6.0 %collective-permute-start.3 = (bf16[3,2,256]{2,1,0:T(2,128)(2,1)S(1)}, bf16[3,2,256]{2,1,0:T(2,128)(2,1)S(1)}, u32[]{:S(2)}, u32[]{:S(2)}) collective-permute-start(bf16[3,2,256]{2,1,0:T(2,128)(2,1)S(1)} %slice.115), channel_id=1, source_target_pairs={{0,4},{4,8},{8,12},{12,16},{16,20},{20,24},{24,28},{1,5},{5,9},{9,... | collective-permute-start | bytes 9224 | tf_op jit(solution)/shard_map/ppermute | solution.py:44
  59.2 6.3 %collective-permute-start.7 = (bf16[2,32,256]{2,1,0:T(8,128)(2,1)S(1)}, bf16[2,32,256]{2,1,0:T(8,128)(2,1)S(1)}, u32[]{:S(2)}, u32[]{:S(2)}) collective-permute-start(bf16[2,32,256]{2,1,0:T(8,128)(2,1)S(1)} %get-tuple-element.36), channel_id=1, source_target_pairs={{0,4},{4,0},{8,12},{12,8},{16,20},{20,16},{24,28},{28,24},{1,5},{5... | collective-permute-start | bytes 98312 | tf_op jit(solution)/shard_map/ppermute | solution.py:34
  60.6 14.3 %collective-permute-start.13 = (bf16[2,32,256]{2,1,0:T(8,128)(2,1)S(1)}, bf16[2,32,256]{2,1,0:T(8,128)(2,1)S(1)}, u32[]{:S(2)}, u32[]{:S(2)}) collective-permute-start(bf16[2,32,256]{2,1,0:T(8,128)(2,1)S(1)} %get-tuple-element.30), channel_id=1, source_target_pairs={{0,28},{4,24},{8,20},{12,16},{16,12},{20,8},{24,4},{28,0},{1,29},{... | collective-permute-start | bytes 98312 | tf_op jit(solution)/shard_map/ppermute | solution.py:34
  62.2 12.2 %collective-permute-start.12 = (bf16[2,32,256]{2,1,0:T(8,128)(2,1)S(1)}, bf16[2,32,256]{2,1,0:T(8,128)(2,1)S(1)}, u32[]{:S(2)}, u32[]{:S(2)}) collective-permute-start(bf16[2,32,256]{2,1,0:T(8,128)(2,1)S(1)} %get-tuple-element.31), channel_id=1, source_target_pairs={{0,24},{4,28},{8,16},{12,20},{16,8},{20,12},{24,0},{28,4},{1,25},{... | collective-permute-start | bytes 98312 | tf_op jit(solution)/shard_map/ppermute | solution.py:34
  63.4 10.4 %collective-permute-start.11 = (bf16[2,32,256]{2,1,0:T(8,128)(2,1)S(1)}, bf16[2,32,256]{2,1,0:T(8,128)(2,1)S(1)}, u32[]{:S(2)}, u32[]{:S(2)}) collective-permute-start(bf16[2,32,256]{2,1,0:T(8,128)(2,1)S(1)} %get-tuple-element.32), channel_id=1, source_target_pairs={{0,20},{4,16},{8,28},{12,24},{16,4},{20,0},{24,12},{28,8},{1,21},{... | collective-permute-start | bytes 98312 | tf_op jit(solution)/shard_map/ppermute | solution.py:34
  65.5 7.7 %collective-permute-start.10 = (bf16[2,32,256]{2,1,0:T(8,128)(2,1)S(1)}, bf16[2,32,256]{2,1,0:T(8,128)(2,1)S(1)}, u32[]{:S(2)}, u32[]{:S(2)}) collective-permute-start(bf16[2,32,256]{2,1,0:T(8,128)(2,1)S(1)} %get-tuple-element.33), channel_id=1, source_target_pairs={{0,16},{4,20},{8,24},{12,28},{16,0},{20,4},{24,8},{28,12},{1,17},{... | collective-permute-start | bytes 98312 | tf_op jit(solution)/shard_map/ppermute | solution.py:34
  65.5 3.1 %collective-permute-start.8 = (bf16[2,32,256]{2,1,0:T(8,128)(2,1)S(1)}, bf16[2,32,256]{2,1,0:T(8,128)(2,1)S(1)}, u32[]{:S(2)}, u32[]{:S(2)}) collective-permute-start(bf16[2,32,256]{2,1,0:T(8,128)(2,1)S(1)} %get-tuple-element.35), channel_id=1, source_target_pairs={{0,8},{4,12},{8,0},{12,4},{16,24},{20,28},{24,16},{28,20},{1,9},{5... | collective-permute-start | bytes 98312 | tf_op jit(solution)/shard_map/ppermute | solution.py:34
  68.5 4.0 %collective-permute-start.9 = (bf16[2,32,256]{2,1,0:T(8,128)(2,1)S(1)}, bf16[2,32,256]{2,1,0:T(8,128)(2,1)S(1)}, u32[]{:S(2)}, u32[]{:S(2)}) collective-permute-start(bf16[2,32,256]{2,1,0:T(8,128)(2,1)S(1)} %get-tuple-element.34), channel_id=1, source_target_pairs={{0,12},{4,8},{8,4},{12,0},{16,28},{20,24},{24,20},{28,16},{1,13},{... | collective-permute-start | bytes 98312 | tf_op jit(solution)/shard_map/ppermute | solution.py:34
  101.0 7.3 %collective-permute-start.24 = (f32[3,2,256]{2,1,0:T(2,128)S(1)}, f32[3,2,256]{2,1,0:T(2,128)S(1)}, u32[]{:S(2)}, u32[]{:S(2)}) collective-permute-start(f32[3,2,256]{2,1,0:T(2,128)S(1)} %slice.136), channel_id=1, source_target_pairs={{4,0},{8,4},{12,8},{16,12},{20,16},{24,20},{28,24},{5,1},{9,5},{13... | collective-permute-start | bytes 18440 | tf_op jit(solution)/shard_map/ppermute | solution.py:44
  104.3 11.6 %collective-permute-start.21 = (bf16[256,256]{1,0:T(8,128)(2,1)S(1)}, bf16[256,256]{1,0:T(8,128)(2,1)S(1)}, u32[]{:S(2)}, u32[]{:S(2)}) collective-permute-start(bf16[256,256]{1,0:T(8,128)(2,1)S(1)} %convolution_convert_fusion.2), channel_id=1, source_target_pairs={{0,1},{1,2},{2,3},{3,0},{4,5},{5,6},{6,7},{7,4},{8,9},{9,10},{10,1... | collective-permute-start | bytes 393224 | tf_op jit(solution)/shard_map/ppermute | solution.py:63
  107.0 17.4 %collective-permute-start.22 = (bf16[256,256]{1,0:T(8,128)(2,1)S(1)}, bf16[256,256]{1,0:T(8,128)(2,1)S(1)}, u32[]{:S(2)}, u32[]{:S(2)}) collective-permute-start(bf16[256,256]{1,0:T(8,128)(2,1)S(1)} %convolution_convert_fusion.1), channel_id=1, source_target_pairs={{0,2},{1,3},{2,0},{3,1},{4,6},{5,7},{6,4},{7,5},{8,10},{9,11},{10,... | collective-permute-start | bytes 393224 | tf_op jit(solution)/shard_map/ppermute | solution.py:63
  108.0 17.3 %collective-permute-start.23 = (bf16[256,256]{1,0:T(8,128)(2,1)S(1)}, bf16[256,256]{1,0:T(8,128)(2,1)S(1)}, u32[]{:S(2)}, u32[]{:S(2)}) collective-permute-start(bf16[256,256]{1,0:T(8,128)(2,1)S(1)} %convolution_convert_fusion), channel_id=1, source_target_pairs={{0,3},{1,0},{2,1},{3,2},{4,7},{5,4},{6,5},{7,6},{8,11},{9,8},{10,9... | collective-permute-start | bytes 393224 | tf_op jit(solution)/shard_map/ppermute | solution.py:63
  109.3 17.9 %collective-permute-start.25 = (bf16[256,256]{1,0:T(8,128)(2,1)S(1)}, bf16[256,256]{1,0:T(8,128)(2,1)S(1)}, u32[]{:S(2)}, u32[]{:S(2)}) collective-permute-start(bf16[256,256]{1,0:T(8,128)(2,1)S(1)} %fusion.30), channel_id=1, source_target_pairs={{0,1},{1,2},{2,3},{3,0},{4,5},{5,6},{6,7},{7,4},{8,9},{9,10},{10,1... | collective-permute-start | bytes 393224 | tf_op jit(solution)/shard_map/ppermute | solution.py:63
  110.5 19.4 %collective-permute-start.26 = (bf16[256,256]{1,0:T(8,128)(2,1)S(1)}, bf16[256,256]{1,0:T(8,128)(2,1)S(1)}, u32[]{:S(2)}, u32[]{:S(2)}) collective-permute-start(bf16[256,256]{1,0:T(8,128)(2,1)S(1)} %fusion.31), channel_id=1, source_target_pairs={{0,2},{1,3},{2,0},{3,1},{4,6},{5,7},{6,4},{7,5},{8,10},{9,11},{10,... | collective-permute-start | bytes 393224 | tf_op jit(solution)/shard_map/ppermute | solution.py:63
  116.0 15.0 %collective-permute-start.27 = (bf16[256,256]{1,0:T(8,128)(2,1)S(1)}, bf16[256,256]{1,0:T(8,128)(2,1)S(1)}, u32[]{:S(2)}, u32[]{:S(2)}) collective-permute-start(bf16[256,256]{1,0:T(8,128)(2,1)S(1)} %fusion.32), channel_id=1, source_target_pairs={{0,3},{1,0},{2,1},{3,2},{4,7},{5,4},{6,5},{7,6},{8,11},{9,8},{10,9... | collective-permute-start | bytes 393224 | tf_op jit(solution)/shard_map/ppermute | solution.py:63
  (23 other events, 187.5 us)
